TPU v7x, 512 devices: a whole 4x8x8 slice. The times are simulated.
512 devices in a mesh: dp: 64 (over x, z, y_lo), fsdp: 8 (over y_hi, core).
Axes of the slice: x: 4, y: 8 (y_hi: 4, y_lo: 2; y = y_hi * 2 + y_lo), z: 8, core: 2. Of those that a mesh axis runs over, the one named last changes fastest.
Arguments:
- group_qkv: bfloat16 [64, 1024, 6144], P('dp', 'fsdp'), may hold values from -6 to 6
- cache_pool: bfloat16 [8192, 16, 4096], P('dp', None, 'fsdp'), may hold values from -6 to 6
- page_request: int32 [8192], P('dp'), may hold values from 0 to 64, as said below
- request_host: int32 [64], replicated, may hold values from 0 to 63, each once
- out_weight: bfloat16 [2048, 2048], P(('dp', 'fsdp')), may hold values from -0.5 to 0.5
Outputs:
- projected: bfloat16 [64, 1024, 2048], P('dp', 'fsdp')
Inputs may be any that keep to these rules, and one draw needn't show every extreme that they name: `page_request`: within the slots of one dp index, at most 2 pages belong to one request, and some request has exactly 2 pages in the slots of every dp index. A request holds 1 to 15 pages, or 64 to 128 pages. Some slot is empty.
All inputs are finite; a program needn't handle non-finite values.
Results may differ from a plain program's by a relative error of at most 0.0053.
Values may be sent and summed in bfloat16 or wider, within the bound.
No kernel may reach another device: no remote copies, remote signals or barrier semaphores. Data moves between devices by JAX's collectives and lax.ppermute only.
A program may use at most 64 MiB of HBM per device.

v0:
```python
import math
import jax
import jax.numpy as jnp
from jax import lax
from jax.sharding import PartitionSpec as P

HD = 128
PAGE = 16
MOST = 2


def per_device(group_qkv, cache_pool, page_request, request_host, out_weight):
    fsdp_count = lax.axis_size("fsdp")
    requests = request_host.shape[0]
    slot_count = page_request.shape[0]
    tokens_here = group_qkv.shape[1]
    features = cache_pool.shape[2]
    heads_here = features // (2 * HD)
    score_scale = 1.0 / math.sqrt(HD)
    request_ids = jnp.arange(requests, dtype=jnp.int32)
    member = (page_request[:, None] == request_ids[None, :]).astype(jnp.int32)
    slot_rank = jnp.sum(member * (jnp.cumsum(member, axis=0) - 1), axis=1)
    target_host = jnp.sum(member * request_host[None, :], axis=1)
    is_live = jnp.sum(member, axis=1)
    target_slot = jnp.where(is_live > 0, target_host * MOST + slot_rank, -1)
    chosen = target_slot[:, None] == jnp.arange(requests * MOST, dtype=jnp.int32)[None, :]
    flat_pool = cache_pool.reshape(slot_count, PAGE * features)
    packed = jnp.einsum(
        "sp,sf->pf", chosen.astype(jnp.bfloat16), flat_pool, preferred_element_type=jnp.float32
    )
    packed = packed.astype(jnp.bfloat16).reshape(requests, MOST, PAGE, features)
    occupied = jnp.sum(chosen.astype(jnp.int32), axis=0).reshape(requests, MOST)
    arrived, present = (
        lax.all_to_all(packed, "dp", split_axis=0, concat_axis=0, tiled=True),
        lax.all_to_all(occupied, "dp", split_axis=0, concat_axis=0, tiled=True),
    )
    cached = arrived.reshape(requests * MOST * PAGE, heads_here, 2, HD)
    key_cache = cached[:, :, 0]
    value_cache = cached[:, :, 1]
    live_tokens = jnp.repeat(present.reshape(requests * MOST), PAGE) > 0
    local_qkv = group_qkv.reshape(tokens_here, fsdp_count, heads_here * 3 * HD)
    gathered_qkv = lax.all_to_all(local_qkv, "fsdp", split_axis=1, concat_axis=0, tiled=True)
    group_len = tokens_here * fsdp_count
    gathered_qkv = gathered_qkv.reshape(group_len, heads_here, 3, HD)
    queries = gathered_qkv[:, :, 0]
    new_keys = gathered_qkv[:, :, 1]
    new_values = gathered_qkv[:, :, 2]
    block_rows = min(512, group_len)
    block_count = group_len // block_rows
    query_blocks = queries.reshape(block_count, block_rows, heads_here, HD)

    def attend(inputs):
        query_block, first_row = inputs
        cache_scores = (
            jnp.einsum("qhd,khd->hqk", query_block, key_cache, preferred_element_type=jnp.float32)
            * score_scale
        )
        cache_scores = jnp.where(live_tokens[None, None, :], cache_scores, -jnp.inf)
        group_scores = (
            jnp.einsum("qhd,khd->hqk", query_block, new_keys, preferred_element_type=jnp.float32)
            * score_scale
        )
        causal = jnp.arange(group_len)[None, :] <= first_row + jnp.arange(block_rows)[:, None]
        group_scores = jnp.where(causal[None, :, :], group_scores, -jnp.inf)
        row_max = jnp.maximum(jnp.max(cache_scores, axis=2), jnp.max(group_scores, axis=2))
        cache_expo = jnp.exp(cache_scores - row_max[:, :, None])
        group_expo = jnp.exp(group_scores - row_max[:, :, None])
        row_total = jnp.sum(cache_expo, axis=2) + jnp.sum(group_expo, axis=2)
        mixture = jnp.einsum(
            "hqk,khd->qhd",
            cache_expo.astype(jnp.bfloat16),
            value_cache,
            preferred_element_type=jnp.float32,
        )
        mixture = mixture + jnp.einsum(
            "hqk,khd->qhd",
            group_expo.astype(jnp.bfloat16),
            new_values,
            preferred_element_type=jnp.float32,
        )
        result = mixture / jnp.transpose(row_total)[:, :, None]
        return result.astype(jnp.bfloat16).reshape(block_rows, heads_here * HD)

    starts = jnp.arange(block_count, dtype=jnp.int32) * block_rows
    attn_heads = lax.map(attend, (query_blocks, starts)).reshape(group_len, heads_here * HD)
    tokens_attn = lax.all_to_all(attn_heads, "fsdp", split_axis=0, concat_axis=1, tiled=True)
    summed = jnp.dot(
        tokens_attn,
        lax.all_gather(out_weight, ("dp", "fsdp"), axis=0, tiled=True),
        preferred_element_type=jnp.float32,
    )
    return summed.astype(jnp.bfloat16).reshape(1, tokens_here, out_weight.shape[1])


def solution(mesh):
    return jax.shard_map(
        per_device,
        mesh=mesh,
        in_specs=(
            P("dp", "fsdp", None),
            P("dp", None, "fsdp"),
            P("dp"),
            P(),
            P(("dp", "fsdp"), None),
        ),
        out_specs=P("dp", "fsdp", None),
        check_vma=False,
    )
```

profile of v0, /device:TPU:10, one launch (start us, length us, event | category | flops | bytes accessed | tf_op | source)
XLA Modules:
  0.0 906.4 jit_solution(7879001282318499317)
XLA Ops:
  8.2 0.9 select_reduce_fusion.1
  9.9 14.8 %all-to-all-start = ((s32[64,1,2]{2,1,0:T(1,128)}), s32[64,1,2]{2,1,0:T(1,128)S(1)}, u32[]{:S(2)}, u32[]{:S(2)}) async-start(s32[64,1,2]{2,1,0:T(1,128)} %bitcast.9), calls=%async_computation | async-start | bytes 65536 | tf_op jit(solution)/shard_map/all_to_all | solution.py:35
  24.7 2.6 copy.34
  27.3 6.0 all-to-all-done
  33.3 6.2 all-to-all-start.1
  39.5 3.0 copy.49
  43.3 2.2 copy.50
  45.5 33.0 %all-to-all-done.1 = bf16[128,8,768]{0,2,1:T(8,128)(2,1)S(1)} async-done(((bf16[128,8,768]{0,2,1:T(8,128)(2,1)}), bf16[128,8,768]{0,2,1:T(8,128)(2,1)S(1)}, u32[]{:S(2)}, u32[]{:S(2)}) %all-to-all-start.1) | async-done | bytes 1572896 | tf_op jit(solution)/shard_map/all_to_all | solution.py:42
  78.5 8.3 all-to-all-start.2
  87.1 1.0 copy.35
  88.9 1.0 slice_bitcast_fusion
  90.4 45.0 %all-to-all-done.2 = bf16[64,2,16,512]{3,2,1,0:T(8,128)(2,1)} async-done(((bf16[64,2,16,512]{3,2,1,0:T(8,128)(2,1)}), bf16[64,2,16,512]{3,2,1,0:T(8,128)(2,1)}, u32[]{:S(2)}, u32[]{:S(2)}) %all-to-all-start.2) | async-done | bytes 2097184 | tf_op jit(solution)/shard_map/all_to_all | solution.py:34
  135.3 2.5 reshape.84
  137.9 3.9 fusion.42
  142.0 5.8 copy.45
  147.8 27.3 %while.11 = (s32[]{:T(128)}, bf16[2,512,256]{2,1,0:T(8,128)(2,1)S(1)}, bf16[2,512,2,128]{3,1,0,2:T(8,128)(2,1)S(1)}, bf16[2048,2,128]{2,0,1:T(8,128)(2,1)S(1)}, ...) while((s32[]{:T(128)}, ...), condition=%wide.region_10.11_spmd.clone, body=%wide.region_5.10_spmd.clone.sunk | while | flops 1646131712 | bytes 69022040 | solution.py:85
  149.4 2.9 fusion.68
  152.5 1.4 fusion.69
  154.7 1.2 fusion.72
  155.9 1.9 fusion.71
  157.8 1.3 fusion.70
  159.1 2.2 fusion.73
  163.1 2.9 fusion.68
  166.2 1.4 fusion.69
  168.4 1.2 fusion.72
  169.5 1.9 fusion.71
  171.5 1.3 fusion.70
  172.8 2.2 fusion.73
  175.1 20.5 %all_to_all.48 = bf16[8,128,256]{2,1,0:T(8,128)(2,1)S(1)} all-to-all(bf16[8,128,256]{2,1,0:T(8,128)(2,1)S(1)} %bitcast.90), channel_id=1, replica_groups=mesh['dp'=64,'fsdp'=8] {'fsdp'}, dimensions={0} | all-to-all | bytes 1048576 | tf_op jit(solution)/shard_map/all_to_all | solution.py:86
  195.9 685.7 %all-gather.3.cloned.1.call-done = bf16[512,4,2048]{2,1,0:T(4,128)(2,1)} async-done(((bf16[1,4,2048]{2,1,0:T(4,128)(2,1)}), bf16[512,4,2048]{2,1,0:T(4,128)(2,1)}) %all-gather.3.cloned.1.call-update) | async-done | bytes 8388624 | tf_op jit(solution)/shard_map/all_gather | solution.py:89
  881.6 12.5 %reshape.87 = bf16[2048,2048]{1,0:T(8,128)(2,1)} reshape(bf16[512,4,2048]{2,1,0:T(4,128)(2,1)} %all-gather.3.cloned.1.call-done) | data formatting | bytes 16777216
  894.1 5.5 fusion.38
  (49 shorter events, 10.7 us)
Async XLA Ops:
  6.5 875.0 %all-gather.3.cloned.1.call-start = ((), (), s32[]{:S(2)}) async-start(), calls=%async_computation.4 | async-start | bytes 8404992 | tf_op jit(solution)/shard_map/all_gather | solution.py:89
  9.9 23.4 %all-to-all-start = ((s32[64,1,2]{2,1,0:T(1,128)}), s32[64,1,2]{2,1,0:T(1,128)S(1)}, u32[]{:S(2)}, u32[]{:S(2)}) async-start(s32[64,1,2]{2,1,0:T(1,128)} %bitcast.9), calls=%async_computation | async-start | bytes 65536 | tf_op jit(solution)/shard_map/all_to_all | solution.py:35
  33.3 45.2 %all-to-all-start.1 = ((bf16[128,8,768]{0,2,1:T(8,128)(2,1)}), bf16[128,8,768]{0,2,1:T(8,128)(2,1)S(1)}, u32[]{:S(2)}, u32[]{:S(2)}) async-start(bf16[128,8,768]{0,2,1:T(8,128)(2,1)} %bitcast), calls=%async_computation.1 | async-start | bytes 3145728 | tf_op jit(solution)/shard_map/all_to_all | solution.py:42
  78.5 56.8 %all-to-all-start.2 = ((bf16[64,2,16,512]{3,2,1,0:T(8,128)(2,1)}), bf16[64,2,16,512]{3,2,1,0:T(8,128)(2,1)}, u32[]{:S(2)}, u32[]{:S(2)}) async-start(bf16[64,2,16,512]{3,2,1,0:T(8,128)(2,1)} %bitcast.29), calls=%async_computation.2 | async-start | bytes 4194304 | tf_op jit(solution)/shard_map/all_to_all | solution.py:34
  141.8 6.0 copy-start.2
  152.5 2.2 copy-start
  155.9 1.9 copy-start.3
  157.8 1.4 copy-start.1
  166.2 2.2 copy-start
  169.5 1.9 copy-start.3
  171.4 1.4 copy-start.1
Sparse Core Ops, SparseCore 0:
  9.5 871.9 all-gather.2
where the time goes:
time: 907 us; the launch traced here: 906 us
  waiting for transfers between devices  770 us (85%)
  local copies, waits for them, and re-layouts  40.5 us (4%)
  starting transfers between devices  29.3 us (3%)
  matrix products  21.8 us (2%)
  blocking collectives  20.5 us (2%)
  between operations  13.5 us (1%)
  other arithmetic  10.2 us (1%)
    all_gather x1, waiting for transfers between devices, per_device(): lax.all_gather(out_weight, ('dp', 'fsdp'), axis=0, tiled=True)  686 us
    all_to_all x1, waiting for transfers between devices, per_device(): lax.all_to_all(packed, 'dp', split_axis=0, concat_axis=0, tiled=True)  45 us
    all_to_all x1, waiting for transfers between devices, per_device(): lax.all_to_all(local_qkv, 'fsdp', split_axis=1, concat_axis=0, tiled=True)  33 us
    all_to_all x1, blocking collectives, per_device(): lax.all_to_all(attn_heads, 'fsdp', split_axis=0, concat_axis=1, tiled=True)  20.5 us
    unnamed x6, local copies, waits for them, and re-layouts  20.3 us
  transfers between devices with their start and end apart: 4, of which 4 were waited for; matrix products, arithmetic and copies ran while one was open for 6% of the time, Pallas kernels for 0%

commit v1 on v0

--- a/solution.py
+++ b/solution.py
@@ -86,7 +86,12 @@
     tokens_attn = lax.all_to_all(attn_heads, "fsdp", split_axis=0, concat_axis=1, tiled=True)
     summed = jnp.dot(
         tokens_attn,
-        lax.all_gather(out_weight, ("dp", "fsdp"), axis=0, tiled=True),
+        jnp.concatenate(
+            lax.all_to_all(
+                jnp.stack([out_weight] * lax.axis_size(("dp", "fsdp"))), ("dp", "fsdp"), 0, 0
+            ),
+            axis=0,
+        ),
         preferred_element_type=jnp.float32,
     )
     return summed.astype(jnp.bfloat16).reshape(1, tokens_here, out_weight.shape[1])

time: 907 us -> 420 us (0.46)
  the two profiles are of different devices: /device:TPU:10 before, /device:TPU:16 now
where the time goes in v1:
time: 420 us; the launch traced here: 419 us
  waiting for transfers between devices  271 us (65%)
  local copies, waits for them, and re-layouts  54.7 us (13%)
  starting transfers between devices  41.5 us (10%)
  matrix products  21.7 us (5%)
  blocking collectives  19 us (5%)
  other arithmetic  10.3 us (2%)
    all_to_all x1, waiting for transfers between devices, per_device(): lax.all_to_all(jnp.stack([out_weight] * lax.axis_size(('dp', 'fsdp'))), (...  187 us
    all_to_all x1, waiting for transfers between devices, per_device(): lax.all_to_all(packed, 'dp', split_axis=0, concat_axis=0, tiled=True)  42.1 us
    all_to_all x1, waiting for transfers between devices, per_device(): lax.all_to_all(local_qkv, 'fsdp', split_axis=1, concat_axis=0, tiled=True)  34.2 us
    all_to_all x1, blocking collectives, per_device(): lax.all_to_all(attn_heads, 'fsdp', split_axis=0, concat_axis=1, tiled=True)  19 us
    all_to_all x1, starting transfers between devices, per_device(): lax.all_to_all(occupied, 'dp', split_axis=0, concat_axis=0, tiled=True)  14.8 us
    all_to_all x1, starting transfers between devices, per_device(): lax.all_to_all(jnp.stack([out_weight] * lax.axis_size(('dp', 'fsdp'))), (...  14.4 us
    reshape x1, local copies, waits for them, and re-layouts, per_device(): jnp.concatenate(lax.all_to_all(jnp.stack([out_weight] * lax.axis_size(('d...  12.5 us
  transfers between devices with their start and end apart: 4, of which 4 were waited for; matrix products, arithmetic and copies ran while one was open for 4% of the time, Pallas kernels for 0%

profile of v1, /device:TPU:16, one launch (start us, length us, event | category | flops | bytes accessed | tf_op | source)
XLA Modules:
  0.0 418.6 jit_solution(11955380357489103725)
XLA Ops:
  2.8 14.8 %all-to-all-start = ((s32[64,1,2]{2,1,0:T(1,128)}), s32[64,1,2]{2,1,0:T(1,128)S(1)}, u32[]{:S(2)}, u32[]{:S(2)}) async-start(s32[64,1,2]{2,1,0:T(1,128)} %bitcast.9), calls=%async_computation | async-start | bytes 65536 | tf_op jit(solution)/shard_map/all_to_all | solution.py:35
  17.6 2.6 copy.34
  20.2 7.7 %all-to-all-done = s32[64,1,2]{2,1,0:T(1,128)S(1)} async-done(((s32[64,1,2]{2,1,0:T(1,128)}), s32[64,1,2]{2,1,0:T(1,128)S(1)}, u32[]{:S(2)}, u32[]{:S(2)}) %all-to-all-start) | async-done | bytes 544 | tf_op jit(solution)/shard_map/all_to_all | solution.py:35
  27.9 6.5 %all-to-all-start.1 = ((bf16[128,8,768]{0,2,1:T(8,128)(2,1)}), bf16[128,8,768]{0,2,1:T(8,128)(2,1)}, u32[]{:S(2)}, u32[]{:S(2)}) async-start(bf16[128,8,768]{0,2,1:T(8,128)(2,1)} %bitcast), calls=%async_computation.1 | async-start | bytes 3145728 | tf_op jit(solution)/shard_map/all_to_all | solution.py:42
  34.5 1.4 copy.49
  36.7 2.1 copy.50
  38.8 34.2 %all-to-all-done.1 = bf16[128,8,768]{0,2,1:T(8,128)(2,1)} async-done(((bf16[128,8,768]{0,2,1:T(8,128)(2,1)}), bf16[128,8,768]{0,2,1:T(8,128)(2,1)}, u32[]{:S(2)}, u32[]{:S(2)}) %all-to-all-start.1) | async-done | bytes 1572896 | tf_op jit(solution)/shard_map/all_to_all | solution.py:42
  73.0 5.7 %all-to-all-start.2 = ((bf16[64,2,16,512]{3,2,1,0:T(8,128)(2,1)}), bf16[64,2,16,512]{3,2,1,0:T(8,128)(2,1)}, u32[]{:S(2)}, u32[]{:S(2)}) async-start(bf16[64,2,16,512]{3,2,1,0:T(8,128)(2,1)} %bitcast.28), calls=%async_computation.2 | async-start | bytes 4194304 | tf_op jit(solution)/shard_map/all_to_all | solution.py:34
  79.0 3.6 copy.35
  82.6 2.5 reshape.86
  86.7 42.1 %all-to-all-done.2 = bf16[64,2,16,512]{3,2,1,0:T(8,128)(2,1)} async-done(((bf16[64,2,16,512]{3,2,1,0:T(8,128)(2,1)}), bf16[64,2,16,512]{3,2,1,0:T(8,128)(2,1)}, u32[]{:S(2)}, u32[]{:S(2)}) %all-to-all-start.2) | async-done | bytes 2097184 | tf_op jit(solution)/shard_map/all_to_all | solution.py:34
  128.8 4.0 reshape.89
  132.8 6.3 %fusion.42 = (bf16[2048,2,1,128]{3,2,1,0:T(2,128)(2,1)}, bf16[2048,2,1,128]{3,2,1,0:T(2,128)(2,1)S(1)}) fusion(bf16[2048,2,2,128]{3,2,1,0:T(2,128)(2,1)} %reshape.89), kind=kLoop, calls=%fused_computation.51 | loop fusion | bytes 4194304 | tf_op jit(solution)/shard_map/slice | solution.py:39
  139.3 5.8 %copy.45 = bf16[2048,2,1,128]{0,3,1,2:T(8,128)(2,1)} copy(bf16[2048,2,1,128]{3,2,1,0:T(2,128)(2,1)} %get-tuple-element.135) | data formatting | bytes 2097152 | tf_op jit(solution)/shard_map/squeeze | solution.py:39
  145.2 27.2 %while.11 = (s32[]{:T(128)}, bf16[2,512,256]{2,1,0:T(8,128)(2,1)S(1)}, bf16[2,512,2,128]{3,1,0,2:T(8,128)(2,1)S(1)}, bf16[2048,2,128]{2,0,1:T(8,128)(2,1)S(1)}, ...) while((s32[]{:T(128)}, ...), condition=%wide.region_10.11_spmd.clone, body=%wide.region_5.10_spmd.clone.sunk | while | flops 1646131712 | bytes 69022040 | solution.py:85
  146.8 2.8 fusion.68
  149.8 1.4 fusion.69
  153.2 1.9 fusion.71
  155.1 1.3 fusion.70
  156.4 2.2 fusion.73
  160.4 2.8 fusion.68
  163.4 1.4 fusion.69
  165.6 1.2 fusion.72
  166.8 1.9 fusion.71
  168.7 1.3 fusion.70
  170.1 2.2 fusion.73
  172.4 19.0 %all_to_all.53 = bf16[8,128,256]{2,1,0:T(8,128)(2,1)S(1)} all-to-all(bf16[8,128,256]{2,1,0:T(8,128)(2,1)S(1)} %bitcast.88), channel_id=1, replica_groups=mesh['dp'=64,'fsdp'=8] {'fsdp'}, dimensions={0} | all-to-all | bytes 1048576 | tf_op jit(solution)/shard_map/all_to_all | solution.py:86
  191.4 7.5 %stack.2 = bf16[512,4,2048]{2,1,0:T(4,128)(2,1)} broadcast(bf16[4,2048]{1,0:T(4,128)(2,1)S(1)} %copy-done.4), dimensions={1,2} | broadcast | bytes 8404992 | tf_op jit(solution)/shard_map/stack | solution.py:91
  198.9 14.4 %all-to-all-start.4 = ((bf16[512,4,2048]{2,1,0:T(4,128)(2,1)}), bf16[512,4,2048]{2,1,0:T(4,128)(2,1)}, u32[]{:S(2)}, u32[]{:S(2)}) async-start(bf16[512,4,2048]{2,1,0:T(4,128)(2,1)} %stack.2), calls=%async_computation.4 | async-start | bytes 16777216 | tf_op jit(solution)/shard_map/all_to_all | solution.py:90
  213.6 187.0 %all-to-all-done.4 = bf16[512,4,2048]{2,1,0:T(4,128)(2,1)} async-done(((bf16[512,4,2048]{2,1,0:T(4,128)(2,1)}), bf16[512,4,2048]{2,1,0:T(4,128)(2,1)}, u32[]{:S(2)}, u32[]{:S(2)}) %all-to-all-start.4) | async-done | bytes 8388640 | tf_op jit(solution)/shard_map/all_to_all | solution.py:90
  400.7 12.5 %reshape.90 = bf16[2048,2048]{1,0:T(8,128)(2,1)} reshape(bf16[512,4,2048]{2,1,0:T(4,128)(2,1)} %all-to-all-done.4) | data formatting | bytes 16777216 | tf_op jit(solution)/shard_map/reshape | solution.py:89
  413.2 5.5 %fusion.38 = bf16[1,128,2048]{2,1,0:T(8,128)(2,1)} fusion(bf16[128,2048]{0,1:T(8,128)(2,1)S(1)} %bitcast.84, bf16[2048,2048]{1,0:T(8,128)(2,1)} %reshape.90), kind=kOutput, calls=%fused_computation.37 | convolution fusion | flops 1074003968 | bytes 9437184 | tf_op jit(solution)/shard_map/dot_general | solution.py:87
  (51 shorter events, 12.5 us)
Async XLA Ops:
  0.0 34.5 %copy-start.1 = (bf16[128,16,512]{2,1,0:T(8,128)(2,1)S(1)}, bf16[128,16,512]{2,1,0:T(8,128)(2,1)}, u32[]{:S(2)}) copy-start(bf16[128,16,512]{2,1,0:T(8,128)(2,1)} %param.8) | copy-start | bytes 6291460
  2.8 25.1 %all-to-all-start = ((s32[64,1,2]{2,1,0:T(1,128)}), s32[64,1,2]{2,1,0:T(1,128)S(1)}, u32[]{:S(2)}, u32[]{:S(2)}) async-start(s32[64,1,2]{2,1,0:T(1,128)} %bitcast.9), calls=%async_computation | async-start | bytes 65536 | tf_op jit(solution)/shard_map/all_to_all | solution.py:35
  27.9 45.0 %all-to-all-start.1 = ((bf16[128,8,768]{0,2,1:T(8,128)(2,1)}), bf16[128,8,768]{0,2,1:T(8,128)(2,1)}, u32[]{:S(2)}, u32[]{:S(2)}) async-start(bf16[128,8,768]{0,2,1:T(8,128)(2,1)} %bitcast), calls=%async_computation.1 | async-start | bytes 3145728 | tf_op jit(solution)/shard_map/all_to_all | solution.py:42
  73.0 55.9 %all-to-all-start.2 = ((bf16[64,2,16,512]{3,2,1,0:T(8,128)(2,1)}), bf16[64,2,16,512]{3,2,1,0:T(8,128)(2,1)}, u32[]{:S(2)}, u32[]{:S(2)}) async-start(bf16[64,2,16,512]{3,2,1,0:T(8,128)(2,1)} %bitcast.28), calls=%async_computation.2 | async-start | bytes 4194304 | tf_op jit(solution)/shard_map/all_to_all | solution.py:34
  145.2 46.3 %copy-start.4 = (bf16[4,2048]{1,0:T(4,128)(2,1)S(1)}, bf16[4,2048]{1,0:T(4,128)(2,1)}, u32[]{:S(2)}) copy-start(bf16[4,2048]{1,0:T(4,128)(2,1)} %param.11) | copy-start | bytes 49156
  149.8 2.2 copy-start
  153.2 1.9 copy-start.3
  155.1 1.4 copy-start.2
  163.4 2.2 copy-start
  166.8 1.9 copy-start.3
  168.7 1.4 copy-start.2
  198.9 201.8 %all-to-all-start.4 = ((bf16[512,4,2048]{2,1,0:T(4,128)(2,1)}), bf16[512,4,2048]{2,1,0:T(4,128)(2,1)}, u32[]{:S(2)}, u32[]{:S(2)}) async-start(bf16[512,4,2048]{2,1,0:T(4,128)(2,1)} %stack.2), calls=%async_computation.4 | async-start | bytes 16777216 | tf_op jit(solution)/shard_map/all_to_all | solution.py:90
